TPU v7x, 512 devices: a whole 4x4x16 slice. The times are simulated.
512 devices in a mesh: smp: 16 (over z), par: 32 (over x, y, core).
Axes of the slice: x: 4, y: 4, z: 16, core: 2. Of those that a mesh axis runs over, the one named last changes fastest.
Arguments:
- jacobian: bfloat16 [4096, 16384], P('smp', 'par'), may hold values from -52 to 52
Outputs:
- panel_factor: float32 [4096, 512], P('smp')
- schur_part: float32 [4096, 4096], P('smp', 'par')
All inputs are finite; a program needn't handle non-finite values.
Results may differ from a plain program's by a relative error of at most 0.0022.
Values may be sent and summed in bfloat16 or wider, within the bound.
No kernel may reach another device: no remote copies, remote signals or barrier semaphores. Data moves between devices by JAX's collectives and lax.ppermute only.
A program may use at most 64 MiB of HBM per device.

v0:
```python
import jax
import jax.numpy as jnp
from jax import lax
from jax.sharding import PartitionSpec as P

PANEL = 512
shift_scale = 0.01


def shards(jacobian):
    row_count, par_width = jacobian.shape
    par_count = lax.axis_size("par")
    smp_count = lax.axis_size("smp")
    sample_total = row_count * smp_count
    param_total = par_width * par_count
    col_width = sample_total // par_count
    row_index = lax.axis_index("smp")
    col_index = lax.axis_index("par")
    widened = jacobian.astype(jnp.float32)
    col_mean = lax.psum(jnp.sum(widened, axis=0), "smp") / sample_total
    centered = (widened - col_mean).astype(jnp.bfloat16)
    gathered = lax.all_gather(centered, "smp", axis=0, tiled=True)
    gram_tile = lax.psum_scatter(
        lax.dot_general(
            gathered, centered, (((1,), (1,)), ((), ())), preferred_element_type=jnp.float32
        )
        / param_total,
        "par",
        scatter_dimension=0,
        tiled=True,
    ).T
    global_rows = row_index * row_count + jnp.arange(row_count, dtype=jnp.int32)
    global_cols = col_index * col_width + jnp.arange(col_width, dtype=jnp.int32)
    diag_mask = global_rows[:, None] == global_cols[None, :]
    trace_total = lax.psum(jnp.sum(jnp.where(diag_mask, gram_tile, 0.0)), ("smp", "par"))
    shift_value = shift_scale * trace_total / sample_total
    shifted = gram_tile + jnp.where(diag_mask, shift_value, 0.0)
    col_keep = (col_index < PANEL // col_width).astype(jnp.float32)
    start_col = jnp.minimum(col_index, PANEL // col_width - 1) * col_width
    placed_rows = lax.dynamic_update_slice(
        jnp.zeros((row_count, PANEL), jnp.float32), shifted * col_keep, (jnp.int32(0), start_col)
    )
    panel_rows = lax.psum(placed_rows, "par")
    row_keep = (row_index < PANEL // row_count).astype(jnp.float32)
    start_row = jnp.minimum(row_index, PANEL // row_count - 1) * row_count
    top_square = lax.dynamic_update_slice(
        jnp.zeros((PANEL, PANEL), jnp.float32), panel_rows * row_keep, (start_row, jnp.int32(0))
    )
    top_band = lax.dynamic_update_slice(
        jnp.zeros((PANEL, col_width), jnp.float32), shifted * row_keep, (start_row, jnp.int32(0))
    )
    square, band_rows = lax.psum((top_square, top_band), "smp")
    factor = jnp.linalg.cholesky(square)
    panel_out = jax.scipy.linalg.solve_triangular(factor, panel_rows.T, lower=True).T
    band_factor = jax.scipy.linalg.solve_triangular(factor, band_rows, lower=True)
    schur_tile = shifted - jnp.dot(panel_out, band_factor, precision=lax.Precision.HIGHEST)
    return (panel_out, schur_tile)


def solution(mesh):
    placed = (P("smp", "par"),)
    return jax.shard_map(
        shards,
        mesh=mesh,
        in_specs=placed,
        out_specs=(P("smp", None), P("smp", "par")),
        check_vma=False,
    )
```

profile of v0, /device:TPU:2, one launch (start us, length us, event | category | flops | bytes accessed | tf_op | source)
XLA Modules:
  0.0 757.3 jit_solution(15600301314958486580)
XLA Ops:
  7.2 1.0 convert_reduce_fusion
  8.2 36.5 %psum.35 = f32[512]{0:T(512)S(1)} all-reduce(f32[512]{0:T(512)S(1)} %convert_reduce_fusion), channel_id=1, replica_groups=mesh['smp'=16,'par'=32] {'smp'}, use_global_device_ids=true, to_apply=%region_1.0 | all-reduce | flops 512 | bytes 4096 | tf_op jit(solution)/shard_map/psum | solution.py:20
  44.7 1.7 fusion.1
  46.5 74.9 %all-gather.2.cloned.1.call-done = bf16[4096,512]{1,0:T(8,128)(2,1)} async-done(((bf16[256,512]{1,0:T(8,128)(2,1)}), bf16[4096,512]{1,0:T(8,128)(2,1)}) %all-gather.2.cloned.1.call-update) | async-done | bytes 4194320 | tf_op jit(solution)/shard_map/all_gather | solution.py:22
  121.4 5.4 convolution_multiply_fusion
  126.9 101.3 %reduce-scatter.2.cloned.1.call-done = f32[128,256]{1,0:T(8,128)} async-done(((f32[4096,256]{1,0:T(8,128)}), f32[128,256]{1,0:T(8,128)}) %reduce-scatter.2.cloned.1.call-update) | async-done | bytes 131088 | tf_op jit(solution)/shard_map/reduce_scatter | solution.py:23
  228.2 1.6 fusion.29
  229.8 101.8 %psum.36 = f32[]{:T(128)} all-reduce(f32[]{:T(128)} %fusion.29), channel_id=1, replica_groups=mesh['smp'=16,'par'=32] {'smp','par'}, use_global_device_ids=true, to_apply=%region_4.5 | all-reduce | flops 1 | bytes 8 | tf_op jit(solution)/shard_map/psum | solution.py:35
  332.3 1.0 multiply_dynamic-update-slice_fusion.1
  333.4 0.8 copy-done.2
  334.2 0.2 all-reduce.7.cloned.1.call-start
  334.4 130.4 %all-reduce.5.cloned.1.call-done = f32[256,512]{0,1:T(8,128)} async-done(((f32[256,512]{0,1:T(8,128)}), f32[256,512]{0,1:T(8,128)}) %all-reduce.5.cloned.1.call-update) | async-done | bytes 524304 | tf_op jit(solution)/shard_map/psum | solution.py:43
  464.7 0.1 broadcast_in_dim.24
  464.9 1.1 multiply_dynamic-update-slice_fusion
  466.0 1.0 copy-done
  467.1 140.6 %all-reduce.7.cloned.1.call-done = (f32[512,512]{0,1:T(8,128)}, f32[512,128]{0,1:T(8,128)}) async-done(((f32[512,512]{0,1:T(8,128)}, f32[512,128]{0,1:T(8,128)}), (f32[512,512]{0,1:T(8,128)}, f32[512,128]{0,1:T(8,128)})) %all-reduce.7.cloned.1.call-update) | async-done | bytes 1310736 | tf_op jit(solution)/shard_map/psum | solution.py:52
  607.7 1.6 copy.3
  609.3 1.4 fusion
  610.7 11.7 %cholesky.103 = f32[128,128]{1,0:T(8,128)S(1)} custom-call(f32[128,128]{1,0:T(8,128)S(1)} %cholesky.263), custom_call_target="Cholesky" | custom-call | tf_op jit(solution)/shard_map/jit(cholesky)/cholesky | solution.py:53
  622.5 9.8 %custom-call.34 = f32[1,128,128]{1,2,0:T(8,128)S(1)} custom-call(f32[1,128,128]{2,1,0:T(8,128)S(1)} %get-tuple-element.35), custom_call_target="InvertDiagBlocksLowerTriangular" | custom-call | tf_op jit(solution)/shard_map/jit(cholesky)/cholesky | solution.py:53
  632.3 0.3 fusion.20
  632.6 0.3 convolution_subtract_fusion
  633.0 11.7 %cholesky.215 = f32[128,128]{1,0:T(8,128)S(1)} custom-call(f32[128,128]{1,0:T(8,128)S(1)} %cholesky.267), custom_call_target="Cholesky" | custom-call | tf_op jit(solution)/shard_map/jit(cholesky)/cholesky | solution.py:53
  644.8 0.1 copy.5
  645.1 0.1 cholesky.222
  645.2 10.0 %custom-call.35 = f32[1,128,128]{1,2,0:T(8,128)S(1)} custom-call(f32[1,128,128]{2,1,0:T(8,128)S(1)} %get-tuple-element.33), custom_call_target="InvertDiagBlocksLowerTriangular" | custom-call | tf_op jit(solution)/shard_map/jit(cholesky)/cholesky | solution.py:53
  655.2 0.3 convolution_dynamic-update-slice_fusion
  655.6 0.6 convolution_subtract_fusion.4
  656.2 11.7 %cholesky.236 = f32[128,128]{1,0:T(8,128)S(1)} custom-call(f32[128,128]{1,0:T(8,128)S(1)} %cholesky.272), custom_call_target="Cholesky" | custom-call | tf_op jit(solution)/shard_map/jit(cholesky)/cholesky | solution.py:53
  668.0 9.8 %custom-call.36 = f32[1,128,128]{1,2,0:T(8,128)S(1)} custom-call(f32[1,128,128]{2,1,0:T(8,128)S(1)} %get-tuple-element.31), custom_call_target="InvertDiagBlocksLowerTriangular" | custom-call | tf_op jit(solution)/shard_map/jit(cholesky)/cholesky | solution.py:53
  677.8 0.3 convolution_dynamic-update-slice_fusion.1
  678.1 0.5 convolution_subtract_fusion.9
  678.6 11.9 %cholesky.253 = f32[128,128]{1,0:T(8,128)S(1)} custom-call(f32[128,128]{1,0:T(8,128)S(1)} %convolution_subtract_fusion.9), custom_call_target="Cholesky" | custom-call | tf_op jit(solution)/shard_map/jit(cholesky)/cholesky | solution.py:53
  690.7 0.7 compare_reduce_fusion.1
  691.4 0.6 compare_reduce_fusion
  692.0 0.7 compare_reduce_fusion.2
  695.2 0.1 select_select_fusion
  695.4 8.8 %while.1 = (s32[]{:T(128)}, f32[512,512]{0,1:T(8,128)S(1)}, s32[4,2]{0,1:T(2,128)S(1)}, f32[4,128,128]{2,1,0:T(8,128)S(1)}, s32[]{:T(128)}) while((s32[]{:T(128)}, f32[512,512]{0,1:T(8,128)S(1)}, s32[4,2]{0,1:T(2,128)S(1)}, f32[4,128,128]{2,1,0:T(8,128)S(1)}, s32[]{:T(128)}) %tuple.30), condition=%wide.while_cond, body=%wide.while_body.sunk | while | flops 2 | bytes 393321 | solution.py:54
  695.5 0.6 fusion.73
  696.1 1.4 dynamic-slice.7
  697.7 0.6 fusion.73
  698.3 1.4 dynamic-slice.7
  699.9 0.6 fusion.73
  700.5 1.4 dynamic-slice.7
  702.1 0.6 fusion.73
  702.6 1.4 dynamic-slice.7
  704.2 39.3 %custom-call.37 = f32[4,128,128]{1,2,0:T(8,128)S(1)} custom-call(f32[4,128,128]{2,1,0:T(8,128)S(1)} %get-tuple-element.9), custom_call_target="InvertDiagBlocksLowerTriangular" | custom-call | tf_op jit(solution)/shard_map/jit(_solve_triangular)/triangular_solve | solution.py:54
  743.5 0.3 fusion.40
  743.8 0.3 convolution_subtract_fusion.7
  744.1 0.3 fusion.47
  744.4 0.4 convolution_subtract_fusion.6
  744.8 0.3 fusion.49
  745.1 0.5 convolution_subtract_fusion.8
  745.6 0.3 fusion.51
  745.9 0.3 fusion.31
  746.2 0.3 convolution_subtract_fusion.5
  746.5 0.3 fusion.48
  746.8 0.4 convolution_subtract_fusion.3
  747.2 0.3 fusion.50
  747.5 0.5 convolution_subtract_fusion.2
  748.1 0.3 fusion.52
  748.4 0.6 convolution_subtract_fusion.1
  749.0 0.8 copy.14
  749.8 1.0 copy.13
  (53 shorter events, 1.6 us)
Async XLA Ops:
  7.2 114.2 %all-gather.2.cloned.1.call-start = ((), (), s32[]{:S(2)}) async-start(), calls=%async_computation.1 | async-start | bytes 4456448 | tf_op jit(solution)/shard_map/all_gather | solution.py:22
  46.5 181.7 %reduce-scatter.2.cloned.1.call-start = ((), (), s32[]{:S(2)}) async-start(), calls=%async_computation.2 | async-start | bytes 4325376 | tf_op jit(solution)/shard_map/reduce_scatter | solution.py:23
  126.8 337.9 %all-reduce.5.cloned.1.call-start = ((), (), s32[]{:S(2)}) async-start(), calls=%async_computation.3 | async-start | bytes 1048576 | tf_op jit(solution)/shard_map/psum | solution.py:43
  333.3 0.8 copy-start.2
  333.4 132.6 %copy-start.3 = (f32[512,128]{0,1:T(8,128)}, f32[512,128]{0,1:T(8,128)S(1)}, u32[]{:S(2)}) copy-start(f32[512,128]{0,1:T(8,128)S(1)} %get-tuple-element.28) | copy-start | bytes 786436
  334.2 273.6 %all-reduce.7.cloned.1.call-start = ((), (), s32[]{:S(2)}) async-start(), calls=%async_computation.4 | async-start | bytes 2621440 | tf_op jit(solution)/shard_map/psum | solution.py:52
  466.0 1.0 copy-start
  645.0 98.5 %copy-start.5 = (f32[512,128]{0,1:T(8,128)S(1)}, f32[512,128]{0,1:T(8,128)}, u32[]{:S(2)}) copy-start(f32[512,128]{0,1:T(8,128)} %get-tuple-element.25) | copy-start | bytes 786436
  655.6 90.3 %copy-start.1 = (f32[256,512]{0,1:T(8,128)S(1)}, f32[256,512]{0,1:T(8,128)}, u32[]{:S(2)}) copy-start(f32[256,512]{0,1:T(8,128)} %all-reduce.5.cloned.1.call-done) | copy-start | bytes 1572868
  695.4 53.0 %copy-start.4 = (f32[128,256]{1,0:T(8,128)S(1)}, f32[128,256]{1,0:T(8,128)}, u32[]{:S(2)}) copy-start(f32[128,256]{1,0:T(8,128)} %reduce-scatter.2.cloned.1.call-done) | copy-start | bytes 393220
Sparse Core Ops, SparseCore 0:
  46.6 74.7 all-gather.1
  126.9 101.1 reduce-scatter.1
  334.3 130.4 all-reduce.4
  467.2 140.4 all-reduce.6
where the time goes:
time: 758 us; the launch traced here: 757 us
  waiting for transfers between devices  447 us (59%)
  blocking collectives  138 us (18%)
  other arithmetic  126 us (17%)
  between operations  17.4 us (2%)
  local copies, waits for them, and re-layouts  14.6 us (2%)
  matrix products  13.1 us (2%)
    psum x1, waiting for transfers between devices, shards(): square, band_rows = lax.psum((top_square, top_band), 'smp')  141 us
    psum x1, waiting for transfers between devices, shards(): panel_rows = lax.psum(placed_rows, 'par')  130 us
    psum x1, blocking collectives, shards(): lax.psum(jnp.sum(jnp.where(diag_mask, gram_tile, 0.0)), ('smp', 'par'))  102 us
    reduce_scatter x1, waiting for transfers between devices, shards(): lax.psum_scatter(lax.dot_general(gathered, centered, (((1,), (1,)), ((),...  101 us
    another operation x14, other arithmetic, shards(): factor = jnp.linalg.cholesky(square)  78.8 us
    all_gather x1, waiting for transfers between devices, shards(): gathered = lax.all_gather(centered, 'smp', axis=0, tiled=True)  74.9 us
    another operation x3, other arithmetic, shards(): jax.scipy.linalg.solve_triangular(factor, panel_rows.T, lower=True)  39.4 us
    psum x1, blocking collectives, shards(): col_mean = lax.psum(jnp.sum(widened, axis=0), 'smp') / sample_total  36.5 us
  transfers between devices with their start and end apart: 4, of which 4 were waited for; matrix products, arithmetic and copies ran while one was open for 0% of the time, Pallas kernels for 0%

commit v1 on v0

--- a/solution.py
+++ b/solution.py
@@ -5,6 +5,19 @@
 
 PANEL = 512
 shift_scale = 0.01
+
+
+def ring_gather(x, axis, dim):
+    ways = lax.axis_size(axis)
+    up = [(d, (d + 1) % ways) for d in range(ways)]
+    down = [(d, (d - 1) % ways) for d in range(ways)]
+    earlier, later = ([x], [x])
+    for _ in range(ways // 2):
+        earlier.append(lax.ppermute(earlier[-1], axis, up))
+    for _ in range((ways - 1) // 2):
+        later.append(lax.ppermute(later[-1], axis, down))
+    line = jnp.concatenate([*earlier[::-1], *later[1:]], axis=dim)
+    return jnp.roll(line, (lax.axis_index(axis) - ways // 2) * x.shape[dim], axis=dim)
 
 
 def shards(jacobian):
@@ -19,7 +32,7 @@
     widened = jacobian.astype(jnp.float32)
     col_mean = lax.psum(jnp.sum(widened, axis=0), "smp") / sample_total
     centered = (widened - col_mean).astype(jnp.bfloat16)
-    gathered = lax.all_gather(centered, "smp", axis=0, tiled=True)
+    gathered = ring_gather(centered, "smp", 0)
     gram_tile = lax.psum_scatter(
         lax.dot_general(
             gathered, centered, (((1,), (1,)), ((), ())), preferred_element_type=jnp.float32

time: 758 us -> 778 us (1.026)
  starting transfers between devices: 0.34 us -> 51.9 us
  waiting for transfers between devices: 447 us -> 402 us
  local copies, waits for them, and re-layouts: 14.6 us -> 23.1 us
    all_gather x1 -> x0, waiting for transfers between devices: 74.9 us -> none  [shards(): gathered = lax.all_gather(centered, 'smp', axis=0, tiled=True)]
    ppermute x0 -> x15, starting transfers between devices: none -> 51.3 us  [the longest x7 36.1 us: ring_gather(): later.append(lax.ppermute(later[-1], axis, down))]
    ppermute x0 -> x15, waiting for transfers between devices: none -> 30.5 us  [the longest x8 30.5 us: ring_gather(): earlier.append(lax.ppermute(earlier[-1], axis, up))]
  transfers between devices with their start and end apart: 4 -> 18, of which waited for: 4 -> 11; matrix products, arithmetic and copies ran while one was open for 0% -> 1% of each run, Pallas kernels for 0% -> 0%
where the time goes in v1:
time: 778 us; the launch traced here: 773 us
  waiting for transfers between devices  402 us (52%)
  blocking collectives  138 us (18%)
  other arithmetic  129 us (17%)
  starting transfers between devices  51.9 us (7%)
  local copies, waits for them, and re-layouts  23.1 us (3%)
  between operations  18.1 us (2%)
  matrix products  10.9 us (1%)
    psum x1, waiting for transfers between devices, shards(): square, band_rows = lax.psum((top_square, top_band), 'smp')  140 us
    psum x1, waiting for transfers between devices, shards(): panel_rows = lax.psum(placed_rows, 'par')  130 us
    psum x1, blocking collectives, shards(): lax.psum(jnp.sum(jnp.where(diag_mask, gram_tile, 0.0)), ('smp', 'par'))  102 us
    reduce_scatter x1, waiting for transfers between devices, shards(): lax.psum_scatter(lax.dot_general(gathered, centered, (((1,), (1,)), ((),...  101 us
    another operation x14, other arithmetic, shards(): factor = jnp.linalg.cholesky(square)  80.2 us
    another operation x3, other arithmetic, shards(): jax.scipy.linalg.solve_triangular(factor, panel_rows.T, lower=True)  40.7 us
    psum x1, blocking collectives, shards(): col_mean = lax.psum(jnp.sum(widened, axis=0), 'smp') / sample_total  36.5 us
    ppermute x7, starting transfers between devices, ring_gather(): later.append(lax.ppermute(later[-1], axis, down))  36.1 us
  transfers between devices with their start and end apart: 18, of which 11 were waited for; matrix products, arithmetic and copies ran while one was open for 1% of the time, Pallas kernels for 0%

profile of v1, /device:TPU:2, one launch (start us, length us, event | category | flops | bytes accessed | tf_op | source)
XLA Modules:
  0.0 773.2 jit_solution(2732795589432317324)
XLA Ops:
  7.2 1.0 convert_reduce_fusion
  8.3 36.5 %psum.35 = f32[512]{0:T(512)S(1)} all-reduce(f32[512]{0:T(512)S(1)} %convert_reduce_fusion), channel_id=1, replica_groups=mesh['smp'=16,'par'=32] {'smp'}, use_global_device_ids=true, to_apply=%region_1.0 | all-reduce | flops 512 | bytes 4096 | tf_op jit(solution)/shard_map/psum | solution.py:33
  44.8 1.0 fusion.2
  45.8 1.9 collective-permute-start
  47.7 10.2 %collective-permute-done = bf16[256,512]{1,0:T(8,128)(2,1)S(1)} collective-permute-done((bf16[256,512]{1,0:T(8,128)(2,1)S(1)}, bf16[256,512]{1,0:T(8,128)(2,1)S(1)}, u32[]{:S(2)}, u32[]{:S(2)}) %collective-permute-start) | collective-permute-done | bytes 262176 | tf_op jit(solution)/shard_map/ppermute | solution.py:16
  57.9 1.9 collective-permute-start.1
  59.8 5.1 collective-permute-start.8
  65.0 4.4 collective-permute-done.1
  69.3 1.9 collective-permute-start.2
  71.3 5.1 collective-permute-start.9
  76.4 3.5 collective-permute-done.2
  79.9 1.9 collective-permute-start.3
  81.8 5.1 collective-permute-start.10
  87.0 2.6 collective-permute-done.3
  89.6 1.9 collective-permute-start.4
  91.5 5.1 collective-permute-start.11
  96.6 2.4 collective-permute-done.4
  99.0 1.9 collective-permute-start.5
  101.0 5.1 collective-permute-start.12
  106.1 2.4 collective-permute-done.5
  108.5 1.9 collective-permute-start.6
  110.4 5.1 collective-permute-start.13
  115.6 2.5 collective-permute-done.6
  118.1 1.9 collective-permute-start.7
  120.0 5.3 collective-permute-start.14
  125.3 2.5 collective-permute-done.7
  127.9 1.0 constant_dynamic-update-slice_fusion.31
  128.8 1.0 constant_dynamic-update-slice_fusion.30
  129.8 1.0 constant_dynamic-update-slice_fusion.29
  130.9 1.0 constant_dynamic-update-slice_fusion.23
  132.1 1.0 constant_dynamic-update-slice_fusion.15
  133.1 1.0 constant_dynamic-update-slice_fusion.14
  134.5 3.2 convolution_multiply_fusion
  137.8 100.7 %reduce-scatter.2.cloned.1.call-done = f32[128,256]{1,0:T(8,128)} async-done(((f32[4096,256]{1,0:T(8,128)}), f32[128,256]{1,0:T(8,128)}) %reduce-scatter.2.cloned.1.call-update) | async-done | bytes 131088 | tf_op jit(solution)/shard_map/reduce_scatter | solution.py:36
  238.6 1.6 fusion.30
  240.2 101.8 %psum.36 = f32[]{:T(128)} all-reduce(f32[]{:T(128)} %fusion.30), channel_id=1, replica_groups=mesh['smp'=16,'par'=32] {'smp','par'}, use_global_device_ids=true, to_apply=%region_4.5 | all-reduce | flops 1 | bytes 8 | tf_op jit(solution)/shard_map/psum | solution.py:48
  342.7 1.0 multiply_dynamic-update-slice_fusion.1
  343.8 0.8 copy-done.3
  345.1 130.1 %all-reduce.5.cloned.1.call-done = f32[256,512]{0,1:T(8,128)} async-done(((f32[256,512]{0,1:T(8,128)}), f32[256,512]{0,1:T(8,128)}) %all-reduce.5.cloned.1.call-update) | async-done | bytes 524304 | tf_op jit(solution)/shard_map/psum | solution.py:56
  475.3 1.1 multiply_dynamic-update-slice_fusion
  476.4 1.0 copy-done
  478.0 140.2 %all-reduce.7.cloned.1.call-done = (f32[512,512]{0,1:T(8,128)}, f32[512,128]{0,1:T(8,128)}) async-done(((f32[512,512]{0,1:T(8,128)}, f32[512,128]{0,1:T(8,128)}), (f32[512,512]{0,1:T(8,128)}, f32[512,128]{0,1:T(8,128)})) %all-reduce.7.cloned.1.call-update) | async-done | bytes 1310736 | tf_op jit(solution)/shard_map/psum | solution.py:65
  618.2 1.6 copy.3
  619.8 1.4 fusion.1
  621.3 11.7 %cholesky.103 = f32[128,128]{1,0:T(8,128)S(1)} custom-call(f32[128,128]{1,0:T(8,128)S(1)} %cholesky.263), custom_call_target="Cholesky" | custom-call | tf_op jit(solution)/shard_map/jit(cholesky)/cholesky | solution.py:66
  633.0 9.8 %custom-call.34 = f32[1,128,128]{1,2,0:T(8,128)S(1)} custom-call(f32[1,128,128]{2,1,0:T(8,128)S(1)} %get-tuple-element.35), custom_call_target="InvertDiagBlocksLowerTriangular" | custom-call | tf_op jit(solution)/shard_map/jit(cholesky)/cholesky | solution.py:66
  643.5 11.7 %cholesky.215 = f32[128,128]{1,0:T(8,128)S(1)} custom-call(f32[128,128]{1,0:T(8,128)S(1)} %cholesky.267), custom_call_target="Cholesky" | custom-call | tf_op jit(solution)/shard_map/jit(cholesky)/cholesky | solution.py:66
  655.2 0.7 select_reduce_fusion.2
  656.3 10.8 %custom-call.35 = f32[1,128,128]{1,2,0:T(8,128)S(1)} custom-call(f32[1,128,128]{2,1,0:T(8,128)} %get-tuple-element.33), custom_call_target="InvertDiagBlocksLowerTriangular" | custom-call | tf_op jit(solution)/shard_map/jit(cholesky)/cholesky | solution.py:66
  668.1 11.7 %cholesky.236 = f32[128,128]{1,0:T(8,128)S(1)} custom-call(f32[128,128]{1,0:T(8,128)S(1)} %cholesky.272), custom_call_target="Cholesky" | custom-call | tf_op jit(solution)/shard_map/jit(cholesky)/cholesky | solution.py:66
  680.0 9.8 %custom-call.36 = f32[1,128,128]{1,2,0:T(8,128)S(1)} custom-call(f32[1,128,128]{2,1,0:T(8,128)S(1)} %get-tuple-element.31), custom_call_target="InvertDiagBlocksLowerTriangular" | custom-call | tf_op jit(solution)/shard_map/jit(cholesky)/cholesky | solution.py:66
  690.6 11.9 %cholesky.253 = f32[128,128]{1,0:T(8,128)S(1)} custom-call(f32[128,128]{1,0:T(8,128)S(1)} %convolution_subtract_fusion.9), custom_call_target="Cholesky" | custom-call | tf_op jit(solution)/shard_map/jit(cholesky)/cholesky | solution.py:66
  702.6 0.7 compare_reduce_fusion.1
  704.0 0.7 compare_reduce_fusion.2
  707.9 11.2 %while.1 = (s32[]{:T(128)}, f32[512,512]{0,1:T(8,128)S(1)}, s32[4,2]{0,1:T(2,128)S(1)}, f32[4,128,128]{2,1,0:T(8,128)}, s32[]{:T(128)}) while((s32[]{:T(128)}, f32[512,512]{0,1:T(8,128)S(1)}, s32[4,2]{0,1:T(2,128)S(1)}, f32[4,128,128]{2,1,0:T(8,128)}, s32[]{:T(128)}) %tuple.30), condition=%wide.while_cond, body=%wide.while_body.sunk | while | flops 2 | bytes 393829 | solution.py:67
  708.5 1.4 dynamic-slice.7
  710.0 0.6 bitcast_dynamic-update-slice_fusion.2
  711.3 1.4 dynamic-slice.7
  712.8 0.6 bitcast_dynamic-update-slice_fusion.2
  714.1 1.4 dynamic-slice.7
  716.9 1.4 dynamic-slice.7
  719.1 40.1 %custom-call.37 = f32[4,128,128]{1,2,0:T(8,128)S(1)} custom-call(f32[4,128,128]{2,1,0:T(8,128)} %get-tuple-element.9), custom_call_target="InvertDiagBlocksLowerTriangular" | custom-call | tf_op jit(solution)/shard_map/jit(_solve_triangular)/triangular_solve | solution.py:67
  764.7 0.8 copy.14
  765.5 1.0 copy.13
  (118 shorter events, 15.9 us)
Async XLA Ops:
  7.2 127.1 %copy-start.1 = (bf16[256,512]{1,0:T(8,128)(2,1)S(1)}, bf16[256,512]{1,0:T(8,128)(2,1)}, u32[]{:S(2)}) copy-start(bf16[256,512]{1,0:T(8,128)(2,1)} %param.1) | copy-start | bytes 786436
  7.2 231.4 %reduce-scatter.2.cloned.1.call-start = ((), (), s32[]{:S(2)}) async-start(), calls=%async_computation.1 | async-start | bytes 4325376 | tf_op jit(solution)/shard_map/reduce_scatter | solution.py:36
  45.8 12.1 %collective-permute-start = (bf16[256,512]{1,0:T(8,128)(2,1)S(1)}, bf16[256,512]{1,0:T(8,128)(2,1)S(1)}, u32[]{:S(2)}, u32[]{:S(2)}) collective-permute-start(bf16[256,512]{1,0:T(8,128)(2,1)S(1)} %fusion.2), channel_id=1, source_target_pairs={{0,32},{32,64},{64,96},{96,128},{128,160},{160,192},{192,224},{224... | collective-permute-start | bytes 786440 | tf_op jit(solution)/shard_map/ppermute | solution.py:16
  57.9 11.4 %collective-permute-start.1 = (bf16[256,512]{1,0:T(8,128)(2,1)S(1)}, bf16[256,512]{1,0:T(8,128)(2,1)S(1)}, u32[]{:S(2)}, u32[]{:S(2)}) collective-permute-start(bf16[256,512]{1,0:T(8,128)(2,1)S(1)} %collective-permute-done), channel_id=1, source_target_pairs={{0,32},{32,64},{64,96},{96,128},{128,160},{160,192},{192,224},{224... | collective-permute-start | bytes 786440 | tf_op jit(solution)/shard_map/ppermute | solution.py:16
  59.8 11.4 %collective-permute-start.8 = (bf16[256,512]{1,0:T(8,128)(2,1)S(1)}, bf16[256,512]{1,0:T(8,128)(2,1)S(1)}, u32[]{:S(2)}, u32[]{:S(2)}) collective-permute-start(bf16[256,512]{1,0:T(8,128)(2,1)S(1)} %fusion.2), channel_id=1, source_target_pairs={{0,480},{32,0},{64,32},{96,64},{128,96},{160,128},{192,160},{224,1... | collective-permute-start | bytes 786440 | tf_op jit(solution)/shard_map/ppermute | solution.py:18
  69.3 10.6 %collective-permute-start.2 = (bf16[256,512]{1,0:T(8,128)(2,1)S(1)}, bf16[256,512]{1,0:T(8,128)(2,1)S(1)}, u32[]{:S(2)}, u32[]{:S(2)}) collective-permute-start(bf16[256,512]{1,0:T(8,128)(2,1)S(1)} %collective-permute-done.1), channel_id=1, source_target_pairs={{0,32},{32,64},{64,96},{96,128},{128,160},{160,192},{192,224},{224... | collective-permute-start | bytes 786440 | tf_op jit(solution)/shard_map/ppermute | solution.py:16
  71.3 10.6 %collective-permute-start.9 = (bf16[256,512]{1,0:T(8,128)(2,1)S(1)}, bf16[256,512]{1,0:T(8,128)(2,1)S(1)}, u32[]{:S(2)}, u32[]{:S(2)}) collective-permute-start(bf16[256,512]{1,0:T(8,128)(2,1)S(1)} %collective-permute-done.8), channel_id=1, source_target_pairs={{0,480},{32,0},{64,32},{96,64},{128,96},{160,128},{192,160},{224,1... | collective-permute-start | bytes 786440 | tf_op jit(solution)/shard_map/ppermute | solution.py:18
  79.9 9.7 %collective-permute-start.3 = (bf16[256,512]{1,0:T(8,128)(2,1)S(1)}, bf16[256,512]{1,0:T(8,128)(2,1)S(1)}, u32[]{:S(2)}, u32[]{:S(2)}) collective-permute-start(bf16[256,512]{1,0:T(8,128)(2,1)S(1)} %collective-permute-done.2), channel_id=1, source_target_pairs={{0,32},{32,64},{64,96},{96,128},{128,160},{160,192},{192,224},{224... | collective-permute-start | bytes 786440 | tf_op jit(solution)/shard_map/ppermute | solution.py:16
  81.8 9.7 %collective-permute-start.10 = (bf16[256,512]{1,0:T(8,128)(2,1)S(1)}, bf16[256,512]{1,0:T(8,128)(2,1)S(1)}, u32[]{:S(2)}, u32[]{:S(2)}) collective-permute-start(bf16[256,512]{1,0:T(8,128)(2,1)S(1)} %collective-permute-done.9), channel_id=1, source_target_pairs={{0,480},{32,0},{64,32},{96,64},{128,96},{160,128},{192,160},{224,1... | collective-permute-start | bytes 786440 | tf_op jit(solution)/shard_map/ppermute | solution.py:18
  89.6 9.5 %collective-permute-start.4 = (bf16[256,512]{1,0:T(8,128)(2,1)S(1)}, bf16[256,512]{1,0:T(8,128)(2,1)S(1)}, u32[]{:S(2)}, u32[]{:S(2)}) collective-permute-start(bf16[256,512]{1,0:T(8,128)(2,1)S(1)} %collective-permute-done.3), channel_id=1, source_target_pairs={{0,32},{32,64},{64,96},{96,128},{128,160},{160,192},{192,224},{224... | collective-permute-start | bytes 786440 | tf_op jit(solution)/shard_map/ppermute | solution.py:16
  91.5 9.5 %collective-permute-start.11 = (bf16[256,512]{1,0:T(8,128)(2,1)S(1)}, bf16[256,512]{1,0:T(8,128)(2,1)S(1)}, u32[]{:S(2)}, u32[]{:S(2)}) collective-permute-start(bf16[256,512]{1,0:T(8,128)(2,1)S(1)} %collective-permute-done.10), channel_id=1, source_target_pairs={{0,480},{32,0},{64,32},{96,64},{128,96},{160,128},{192,160},{224,1... | collective-permute-start | bytes 786440 | tf_op jit(solution)/shard_map/ppermute | solution.py:18
  99.0 9.5 %collective-permute-start.5 = (bf16[256,512]{1,0:T(8,128)(2,1)S(1)}, bf16[256,512]{1,0:T(8,128)(2,1)S(1)}, u32[]{:S(2)}, u32[]{:S(2)}) collective-permute-start(bf16[256,512]{1,0:T(8,128)(2,1)S(1)} %collective-permute-done.4), channel_id=1, source_target_pairs={{0,32},{32,64},{64,96},{96,128},{128,160},{160,192},{192,224},{224... | collective-permute-start | bytes 786440 | tf_op jit(solution)/shard_map/ppermute | solution.py:16
  101.0 9.5 %collective-permute-start.12 = (bf16[256,512]{1,0:T(8,128)(2,1)S(1)}, bf16[256,512]{1,0:T(8,128)(2,1)S(1)}, u32[]{:S(2)}, u32[]{:S(2)}) collective-permute-start(bf16[256,512]{1,0:T(8,128)(2,1)S(1)} %collective-permute-done.11), channel_id=1, source_target_pairs={{0,480},{32,0},{64,32},{96,64},{128,96},{160,128},{192,160},{224,1... | collective-permute-start | bytes 786440 | tf_op jit(solution)/shard_map/ppermute | solution.py:18
  108.5 1.9 copy-start.5
  108.5 9.6 %collective-permute-start.6 = (bf16[256,512]{1,0:T(8,128)(2,1)S(1)}, bf16[256,512]{1,0:T(8,128)(2,1)}, u32[]{:S(2)}, u32[]{:S(2)}) collective-permute-start(bf16[256,512]{1,0:T(8,128)(2,1)S(1)} %collective-permute-done.5), channel_id=1, source_target_pairs={{0,32},{32,64},{64,96},{96,128},{128,160},{160,192},{192,224},{224... | collective-permute-start | bytes 786440 | tf_op jit(solution)/shard_map/ppermute | solution.py:16
  110.4 9.6 %collective-permute-start.13 = (bf16[256,512]{1,0:T(8,128)(2,1)S(1)}, bf16[256,512]{1,0:T(8,128)(2,1)S(1)}, u32[]{:S(2)}, u32[]{:S(2)}) collective-permute-start(bf16[256,512]{1,0:T(8,128)(2,1)S(1)} %collective-permute-done.12), channel_id=1, source_target_pairs={{0,480},{32,0},{64,32},{96,64},{128,96},{160,128},{192,160},{224,1... | collective-permute-start | bytes 786440 | tf_op jit(solution)/shard_map/ppermute | solution.py:18
  118.1 9.8 %collective-permute-start.7 = (bf16[256,512]{1,0:T(8,128)(2,1)}, bf16[256,512]{1,0:T(8,128)(2,1)}, u32[]{:S(2)}, u32[]{:S(2)}) collective-permute-start(bf16[256,512]{1,0:T(8,128)(2,1)} %collective-permute-done.6), channel_id=1, source_target_pairs={{0,32},{32,64},{64,96},{96,128},{128,160},{160,192},{192,224},{224... | collective-permute-start | bytes 786440 | tf_op jit(solution)/shard_map/ppermute | solution.py:16
  120.0 14.0 %copy-start.6 = (bf16[256,512]{1,0:T(8,128)(2,1)S(1)}, bf16[256,512]{1,0:T(8,128)(2,1)}, u32[]{:S(2)}) copy-start(bf16[256,512]{1,0:T(8,128)(2,1)} %copy-done.5) | copy-start | bytes 786436
  120.0 12.0 %collective-permute-start.14 = (bf16[256,512]{1,0:T(8,128)(2,1)S(1)}, bf16[256,512]{1,0:T(8,128)(2,1)S(1)}, u32[]{:S(2)}, u32[]{:S(2)}) collective-permute-start(bf16[256,512]{1,0:T(8,128)(2,1)S(1)} %collective-permute-done.13), channel_id=1, source_target_pairs={{0,480},{32,0},{64,32},{96,64},{128,96},{160,128},{192,160},{224,1... | collective-permute-start | bytes 786440 | tf_op jit(solution)/shard_map/ppermute | solution.py:18
  137.7 337.4 %all-reduce.5.cloned.1.call-start = ((), (), s32[]{:S(2)}) async-start(), calls=%async_computation.2 | async-start | bytes 1048576 | tf_op jit(solution)/shard_map/psum | solution.py:56
  343.7 0.8 copy-start.3
  343.8 132.7 %copy-start.4 = (f32[512,128]{0,1:T(8,128)}, f32[512,128]{0,1:T(8,128)S(1)}, u32[]{:S(2)}) copy-start(f32[512,128]{0,1:T(8,128)S(1)} %get-tuple-element.28) | copy-start | bytes 786436
  344.6 273.6 %all-reduce.7.cloned.1.call-start = ((), (), s32[]{:S(2)}) async-start(), calls=%async_computation.3 | async-start | bytes 2621440 | tf_op jit(solution)/shard_map/psum | solution.py:65
  476.4 1.0 copy-start
  618.2 141.1 %copy-start.8 = (f32[512,128]{0,1:T(8,128)S(1)}, f32[512,128]{0,1:T(8,128)}, u32[]{:S(2)}) copy-start(f32[512,128]{0,1:T(8,128)} %get-tuple-element.25) | copy-start | bytes 786436
  618.2 143.4 %copy-start.2 = (f32[256,512]{0,1:T(8,128)S(1)}, f32[256,512]{0,1:T(8,128)}, u32[]{:S(2)}) copy-start(f32[256,512]{0,1:T(8,128)} %all-reduce.5.cloned.1.call-done) | copy-start | bytes 1572868
  621.3 142.9 %copy-start.7 = (f32[128,256]{1,0:T(8,128)S(1)}, f32[128,256]{1,0:T(8,128)}, u32[]{:S(2)}) copy-start(f32[128,256]{1,0:T(8,128)} %reduce-scatter.2.cloned.1.call-done) | copy-start | bytes 393220
Sparse Core Ops, SparseCore 0:
  137.8 100.6 reduce-scatter.1
  344.7 130.4 all-reduce.4
  477.6 140.5 all-reduce.6
